TPU v7x, 512 devices: a whole 4x8x8 slice. The times are simulated.
512 devices in a mesh: ctx: 32 (over z, x), tp: 16 (over y, core).
Axes of the slice: x: 4, y: 8, z: 8, core: 2. Of those that a mesh axis runs over, the one named last changes fastest.
Arguments:
- hidden: bfloat16 [8192, 2048], P(('ctx', 'tp')), may hold values from -14 to 14
- in_weight: bfloat16 [2048, 2, 4096], P(None, None, 'tp'), may hold values from -0.125 to 0.125
- step_weight: bfloat16 [2048, 64], P(None, 'tp'), may hold values from -0.125 to 0.125
- group_weight: bfloat16 [256, 4, 2048], P('tp'), may hold values from -0.125 to 0.125
- conv_inner: float32 [4, 4096], P(None, 'tp'), may hold values from -3 to 3
- inner_bias: float32 [4096], P('tp'), may hold values from -2.5 to 2.5
- conv_group: float32 [4, 1024], replicated, may hold values from -3 to 3
- group_bias: float32 [1024], replicated, may hold values from -2.5 to 2.5
- step_bias: float32 [64], P('tp'), may hold values from -9.5 to 0
- log_rate: float32 [64], P('tp'), may hold values from -2.5 to -0.5
- skip_weight: float32 [64], P('tp'), may hold values from 0.25 to 1
- norm_gain: float32 [4096], P('tp'), may hold values from 0.1 to 1.9
- out_weight: bfloat16 [4096, 2048], P('tp'), may hold values from -0.09375 to 0.09375
Outputs:
- mixed: bfloat16 [8192, 2048], P(('ctx', 'tp'))
All inputs are finite; a program needn't handle non-finite values.
Results may differ from a plain program's by a relative error of at most 0.024.
Values may be sent and summed in bfloat16 or wider, within the bound.
No kernel may reach another device: no remote copies, remote signals or barrier semaphores. Data moves between devices by JAX's collectives and lax.ppermute only.
A program may use at most 64 MiB of HBM per device.

v0:
```python
import jax
import jax.numpy as jnp
from jax import lax
from jax.sharding import PartitionSpec as P

HEADS = 64
HEAD_DIM = 64
STATE = 128
GROUPS = 4
BLOCK = 256
KERNEL = 4


def shifted(x, axis, by):
    peers = lax.axis_size(axis)
    pairs = [(i, i + by) for i in range(peers) if 0 <= i + by < peers]
    return lax.ppermute(x, axis, pairs)


def entering(x, axis, combine, identity):
    peers, place = (lax.axis_size(axis), lax.axis_index(axis))
    everything = jax.tree.map(lambda part: lax.all_gather(part, axis), x)
    start = jax.tree.map(
        lambda part, zero: jnp.broadcast_to(jnp.asarray(zero, part.dtype), part.shape), x, identity
    )

    def turn(k, before):
        reached = k < place
        new = combine(before, jax.tree.map(lambda part: part[k], everything))
        return jax.tree.map(lambda a, b: jnp.where(reached, a, b), new, before)

    return lax.fori_loop(0, peers, turn, start)


def causal_conv(prior_rows, raw_rows, conv_weight, conv_bias):
    joined = jnp.concatenate([prior_rows, raw_rows], axis=0).astype(jnp.float32)
    length = raw_rows.shape[0]
    running = jnp.broadcast_to(conv_bias[None, :], raw_rows.shape)
    for offset in range(conv_weight.shape[0]):
        running = running + conv_weight[offset][None, :] * joined[offset : offset + length]
    return jax.nn.silu(running).astype(jnp.bfloat16)


def combine_states(earlier, latter):
    return (earlier[0] * latter[0], latter[0][:, None, None] * earlier[1] + latter[1])


def body(
    hidden,
    in_weight,
    step_weight,
    group_weight,
    conv_inner,
    inner_bias,
    conv_group,
    group_bias,
    step_bias,
    log_rate,
    skip_weight,
    norm_gain,
    out_weight,
):
    heads_dev = log_rate.shape[0]
    inner_dev = in_weight.shape[2]
    group_cols = 2 * STATE
    group_index = lax.axis_index("tp") * heads_dev // (HEADS // GROUPS)
    zx_weight = in_weight.reshape(in_weight.shape[0], 2 * inner_dev)
    full_weight = lax.all_gather(group_weight, "tp", axis=0, tiled=True)
    map_weight = lax.dynamic_slice_in_dim(full_weight, group_index, 1, 1)[:, 0, :]
    shard_rows = lax.all_gather(hidden, "tp", axis=0, tiled=True)
    projected = jnp.concatenate(
        [
            jnp.dot(shard_rows, zx_weight, preferred_element_type=jnp.float32),
            lax.dot_general(
                shard_rows, map_weight, (((1,), (1,)), ((), ())), preferred_element_type=jnp.float32
            ),
            jnp.dot(shard_rows, step_weight, preferred_element_type=jnp.float32),
        ],
        axis=1,
    ).astype(jnp.bfloat16)
    gate_raw = projected[:, :inner_dev]
    inner_raw = projected[:, inner_dev : 2 * inner_dev]
    map_part = projected[:, 2 * inner_dev : projected.shape[1] - heads_dev]
    step_raw = projected[:, projected.shape[1] - heads_dev :]
    border_rows = KERNEL - 1
    length = inner_raw.shape[0]
    inner_prior, map_prior = shifted(
        (inner_raw[length - border_rows :], map_part[length - border_rows :]), "ctx", 1
    )
    x_conv = causal_conv(inner_prior, inner_raw, conv_inner, inner_bias)
    own_taps = lax.dynamic_slice_in_dim(conv_group, group_index * group_cols, group_cols, 1)
    own_bias = lax.dynamic_slice_in_dim(group_bias, group_index * group_cols, group_cols, 0)
    maps = causal_conv(map_prior, map_part, own_taps, own_bias)
    step_size = jax.nn.softplus(step_raw.astype(jnp.float32) + step_bias[None, :])
    decay_rate = -jnp.exp(log_rate)
    blocks = length // BLOCK
    x_blocks = x_conv.reshape(blocks, BLOCK, heads_dev, HEAD_DIM)
    input_map = maps[:, :STATE].reshape(blocks, BLOCK, STATE)
    output_map = maps[:, STATE:].reshape(blocks, BLOCK, STATE)
    step_blocks = jnp.swapaxes(step_size.reshape(blocks, BLOCK, heads_dev), 1, 2)
    cumulative = jnp.cumsum(step_blocks * decay_rate[None, :, None], axis=2)
    scores = jnp.einsum("kin,kjn->kij", output_map, input_map, preferred_element_type=jnp.float32)
    causal = jnp.arange(BLOCK)[:, None] >= jnp.arange(BLOCK)[None, :]
    exponent = jnp.where(causal, cumulative[..., :, None] - cumulative[..., None, :], -jnp.inf)
    mixing = (scores[:, None] * jnp.exp(exponent) * step_blocks[..., None, :]).astype(jnp.bfloat16)
    within = jnp.einsum("khij,kjhp->kihp", mixing, x_blocks, preferred_element_type=jnp.float32)
    weight = jnp.exp(cumulative[..., BLOCK - 1 :] - cumulative) * step_blocks
    x_float = x_blocks.astype(jnp.float32)
    weighted = (x_float * jnp.swapaxes(weight, 1, 2)[..., None]).astype(jnp.bfloat16)
    block_state = jnp.einsum(
        "kjhp,kjn->khpn", weighted, input_map, preferred_element_type=jnp.float32
    )
    block_decay = jnp.exp(cumulative[..., BLOCK - 1])

    def advance(carry, item):
        running, product = carry
        block_stop_index, state_here = item
        return (
            (block_stop_index[:, None, None] * running + state_here, product * block_stop_index),
            (running, product),
        )

    empty_state = jnp.zeros((heads_dev, HEAD_DIM, STATE), jnp.float32)
    (dev_state, dev_decay), (local_starts, prefixes) = lax.scan(
        advance, (empty_state, jnp.ones((heads_dev,), jnp.float32)), (block_decay, block_state)
    )
    decay_in, incoming = entering(
        (dev_decay, dev_state),
        "ctx",
        combine_states,
        (jnp.ones_like(dev_decay), jnp.zeros_like(dev_state)),
    )
    starting = local_starts + prefixes[:, :, None, None] * incoming[None]
    carried = jnp.einsum(
        "kin,khpn->kihp",
        output_map,
        starting.astype(jnp.bfloat16),
        preferred_element_type=jnp.float32,
    )
    carried = carried * jnp.swapaxes(jnp.exp(cumulative), 1, 2)[..., None]
    result_heads = within + carried + skip_weight[None, None, :, None] * x_float
    result_heads = result_heads.reshape(length, inner_dev)
    gated = result_heads * jax.nn.silu(gate_raw.astype(jnp.float32))
    squares = jnp.sum(gated * gated, axis=1)
    own_slot = (jnp.arange(GROUPS) == group_index)[:, None]
    group_sums = lax.psum(jnp.where(own_slot, squares[None, :], 0.0), "tp")
    own_total = jnp.sum(jnp.where(own_slot, group_sums, 0.0), axis=0)
    inverse = lax.rsqrt(own_total / (HEADS * HEAD_DIM // GROUPS) + 1e-05)
    normed = (gated * inverse[:, None] * norm_gain[None, :]).astype(jnp.bfloat16)
    mixed = lax.psum_scatter(
        jnp.dot(normed, out_weight, preferred_element_type=jnp.float32),
        "tp",
        scatter_dimension=0,
        tiled=True,
    )
    return mixed.astype(jnp.bfloat16)


def solution(mesh):
    placed = (
        P(("ctx", "tp"), None),
        P(None, None, "tp"),
        P(None, "tp"),
        P("tp", None, None),
        P(None, "tp"),
        P("tp"),
        P(),
        P(),
        P("tp"),
        P("tp"),
        P("tp"),
        P("tp"),
        P("tp", None),
    )
    return jax.shard_map(
        body, mesh=mesh, in_specs=placed, out_specs=P(("ctx", "tp"), None), check_vma=False
    )
```

profile of v0, /device:TPU:27, one launch (start us, length us, event | category | flops | bytes accessed | tf_op | source)
XLA Modules:
  0.0 323.9 jit_solution(4867282855328708421)
XLA Ops:
  6.5 0.7 all-gather.6.cloned.1.call-update
  7.3 1.8 copy.45
  9.3 2.1 copy.56
  11.3 0.8 dynamic_slice.29
  12.1 0.9 constant_dynamic-slice_fusion
  13.1 41.7 %all-gather.6.cloned.1.call-done = bf16[256,2048]{1,0:T(8,128)(2,1)} async-done(((bf16[16,2048]{1,0:T(8,128)(2,1)}), bf16[256,2048]{1,0:T(8,128)(2,1)}) %all-gather.6.cloned.1.call-update) | async-done | bytes 1048592 | tf_op jit(solution)/shard_map/all_gather | solution.py:70
  54.8 1.6 bitcast_multiply_fusion.1
  56.4 1.2 reduce-window.6
  58.1 1.9 convolution_convert_fusion
  60.1 3.1 collective-permute-start
  63.2 0.2 slice_reduce_fusion
  63.5 0.1 copy.50
  63.6 0.8 collective-permute-done
  64.4 35.8 %all-gather.8.cloned.1.call-done = bf16[256,4,2048]{2,0,1:T(8,128)(2,1)} async-done(((bf16[16,4,2048]{2,0,1:T(8,128)(2,1)}), bf16[256,4,2048]{2,0,1:T(8,128)(2,1)}) %all-gather.8.cloned.1.call-update) | async-done | bytes 4194320 | tf_op jit(solution)/shard_map/all_gather | solution.py:68
  100.3 2.0 fusion.4
  102.3 3.1 collective-permute-start.1
  105.4 0.2 multiply_convert_fusion.3
  105.7 0.9 collective-permute-done.1
  106.6 0.2 multiply_convert_fusion.4
  106.8 0.8 convolution_add_fusion
  107.9 34.2 %all-gather = f32[32,4,1]{1,2,0:T(1,128)S(1)} all-gather(f32[1,4,1]{1,2,0:T(1,128)S(1)} %copy.48), channel_id=2, replica_groups=mesh['ctx'=32,'tp'=16] {'ctx'}, dimensions={0}, use_global_device_ids=true | all-gather | bytes 528 | tf_op jit(solution)/shard_map/all_gather | solution.py:22
  142.4 0.2 fusion.34
  142.6 49.1 %all-gather.10.cloned.1.call-done = f32[128,64,128]{2,1,0:T(8,128)} async-done(((f32[4,64,128]{2,1,0:T(8,128)}), f32[128,64,128]{2,1,0:T(8,128)}) %all-gather.10.cloned.1.call-update) | async-done | bytes 4194320 | tf_op jit(solution)/shard_map/all_gather | solution.py:22
  191.7 33.1 %while.9 = (s32[]{:T(128)}, f32[4,64,128]{2,1,0:T(8,128)S(1)}, s32[]{:T(128)}, f32[32,4]{1,0:T(8,128)S(1)}, f32[32,4,64,128]{3,2,1,0:T(8,128)}, /*index=5*/s32[]{:T(128)}, s32[]{:T(128)}) while((s32[]{:T(128)}, f32[4,64,128]{2,1,0:T(8,128)S(1)}, s32[]{:T(128)}, f32[32,4]{1,0:T(8,128)S(1)}, f32[32,4,64,128]{3,2,1,0:T(8,128)}, ...), condition=%wide.region_3.4_spmd.clone, body=%wide.region_2.3_spmd.clone.sunk | while | flops 131076 | bytes 393369 | solution.py:32
  191.7 1.0 fusion.52
  192.7 1.0 fusion.52
  193.8 1.0 fusion.52
  194.8 1.0 fusion.52
  195.8 1.0 fusion.52
  196.9 1.0 fusion.52
  197.9 1.0 fusion.52
  198.9 1.0 fusion.52
  200.0 1.0 fusion.52
  201.0 1.0 fusion.52
  202.0 1.0 fusion.52
  203.1 1.0 fusion.52
  204.1 1.0 fusion.52
  205.1 1.0 fusion.52
  206.2 1.0 fusion.52
  207.2 1.0 fusion.52
  208.2 1.0 fusion.52
  209.3 1.0 fusion.52
  210.3 1.0 fusion.52
  211.3 1.0 fusion.52
  212.4 1.0 fusion.52
  213.4 1.0 fusion.52
  214.5 1.0 fusion.52
  215.5 1.0 fusion.52
  216.5 1.0 fusion.52
  217.6 1.0 fusion.52
  218.6 1.0 fusion.52
  219.6 1.0 fusion.52
  220.7 1.0 fusion.52
  221.7 1.0 fusion.52
  222.7 1.0 fusion.52
  223.8 1.0 fusion.52
  224.8 0.2 fusion.1
  225.0 0.5 fusion.3
  225.5 0.1 copy.54
  225.6 0.2 multiply_reduce_fusion
  225.8 26.8 %psum.7 = f32[4,256]{1,0:T(4,128)S(1)} all-reduce(f32[4,256]{1,0:T(4,128)S(1)} %broadcast_select_fusion), channel_id=1, replica_groups=mesh['ctx'=32,'tp'=16] {'tp'}, use_global_device_ids=true, to_apply=%region_5.6 | all-reduce | flops 1024 | bytes 8192 | tf_op jit(solution)/shard_map/psum | solution.py:146
  252.8 1.8 fusion.27
  254.7 61.1 %reduce-scatter.2.cloned.1.call-done = f32[16,2048]{1,0:T(8,128)} async-done(((f32[256,2048]{1,0:T(8,128)}), f32[16,2048]{1,0:T(8,128)}) %reduce-scatter.2.cloned.1.call-update) | async-done | bytes 131088 | tf_op jit(solution)/shard_map/reduce_scatter | solution.py:150
  315.8 1.5 convert_element_type.77
  (87 shorter events, 1.8 us)
Async XLA Ops:
  6.5 246.2 %copy-start = (bf16[256,2048]{1,0:T(8,128)(2,1)S(1)}, bf16[256,2048]{1,0:T(8,128)(2,1)}, u32[]{:S(2)}) copy-start(bf16[256,2048]{1,0:T(8,128)(2,1)} %param.27) | copy-start | bytes 3145732
  6.5 48.3 %all-gather.6.cloned.1.call-start = ((), (), s32[]{:S(2)}) async-start(), calls=%async_computation.1 | async-start | bytes 1114112 | tf_op jit(solution)/shard_map/all_gather | solution.py:70
  7.3 93.0 %all-gather.8.cloned.1.call-start = ((), (), s32[]{:S(2)}) async-start(), calls=%async_computation.2 | async-start | bytes 4456448 | tf_op jit(solution)/shard_map/all_gather | solution.py:68
  9.2 182.5 %all-gather.10.cloned.1.call-start = ((), (), s32[]{:S(2)}) async-start(), calls=%async_computation.4 | async-start | bytes 4325376 | tf_op jit(solution)/shard_map/all_gather | solution.py:22
  9.2 3.8 %copy-start.5 = (f32[4]{0:T(128)S(1)}, f32[4]{0:T(128)}, u32[]{:S(2)}) copy-start(f32[4]{0:T(128)} %param.24) | copy-start | bytes 52
  9.2 3.8 %copy-start.1 = (f32[4,256]{1,0:T(4,128)S(1)}, f32[4,256]{1,0:T(4,128)}, u32[]{:S(2)}) copy-start(f32[4,256]{1,0:T(4,128)} %param.19) | copy-start | bytes 12292
  9.3 45.5 %copy-start.4 = (bf16[2048,4]{0,1:T(4,128)(2,1)S(1)}, bf16[2048,4]{0,1:T(4,128)(2,1)}, u32[]{:S(2)}) copy-start(bf16[2048,4]{0,1:T(4,128)(2,1)} %param.17) | copy-start | bytes 49156
  9.3 45.5 %copy-start.6 = (f32[4]{0:T(128)S(1)}, f32[4]{0:T(128)}, u32[]{:S(2)}) copy-start(f32[4]{0:T(128)} %param.23) | copy-start | bytes 52
  60.0 45.4 %copy-start.3 = (f32[256]{0:T(256)S(1)}, f32[256]{0:T(256)}, u32[]{:S(2)}) copy-start(f32[256]{0:T(256)} %param.20) | copy-start | bytes 3076
  60.1 4.3 %collective-permute-start = (bf16[3,256]{1,0:T(4,128)(2,1)S(1)}, bf16[3,256]{1,0:T(4,128)(2,1)S(1)}, u32[]{:S(2)}, u32[]{:S(2)}) collective-permute-start(bf16[3,256]{1,0:T(4,128)(2,1)S(1)} %slice.112), channel_id=1, source_target_pairs={{0,16},{16,32},{32,48},{48,64},{64,80},{80,96},{96,112},{112,128},... | collective-permute-start | bytes 4616 | tf_op jit(solution)/shard_map/ppermute | solution.py:17
  102.3 4.3 %collective-permute-start.1 = (bf16[3,256]{1,0:T(4,128)(2,1)S(1)}, bf16[3,256]{1,0:T(4,128)(2,1)S(1)}, u32[]{:S(2)}, u32[]{:S(2)}) collective-permute-start(bf16[3,256]{1,0:T(4,128)(2,1)S(1)} %slice.118), channel_id=1, source_target_pairs={{0,16},{16,32},{32,48},{48,64},{64,80},{80,96},{96,112},{112,128},... | collective-permute-start | bytes 4616 | tf_op jit(solution)/shard_map/ppermute | solution.py:17
  106.8 118.1 %copy-start.7 = (f32[4]{0:T(128)S(1)}, f32[4]{0:T(128)}, u32[]{:S(2)}) copy-start(f32[4]{0:T(128)} %param.25) | copy-start | bytes 52
  107.7 208.1 %reduce-scatter.2.cloned.1.call-start = ((), (), s32[]{:S(2)}) async-start(), calls=%async_computation.3 | async-start | bytes 2228224 | tf_op jit(solution)/shard_map/reduce_scatter | solution.py:150
  224.8 28.0 %copy-start.2 = (f32[256]{0:T(256)S(1)}, f32[256]{0:T(256)}, u32[]{:S(2)}) copy-start(f32[256]{0:T(256)} %param.26) | copy-start | bytes 3076
Sparse Core Ops, SparseCore 0:
  9.5 45.2 all-gather.5
  56.9 43.2 all-gather.7
  107.8 83.8 all-gather.9
  254.8 60.9 reduce-scatter.1
where the time goes:
time: 325 us; the launch traced here: 324 us
  waiting for transfers between devices  190 us (58%)
  blocking collectives  61.1 us (19%)
  other arithmetic  35.5 us (11%)
  between operations  13.5 us (4%)
  matrix products  9.08 us (3%)
  local copies, waits for them, and re-layouts  7.25 us (2%)
  starting transfers between devices  6.32 us (2%)
    reduce_scatter x1, waiting for transfers between devices, body(): lax.psum_scatter(jnp.dot(normed, out_weight, preferred_element_type=jnp.f...  61.1 us
    all_gather x1, waiting for transfers between devices, entering(): everything = jax.tree.map(lambda part: lax.all_gather(part, axis), x)  49.1 us
    all_gather x1, waiting for transfers between devices, body(): shard_rows = lax.all_gather(hidden, 'tp', axis=0, tiled=True)  41.7 us
    all_gather x1, waiting for transfers between devices, body(): full_weight = lax.all_gather(group_weight, 'tp', axis=0, tiled=True)  35.8 us
    all_gather x1, blocking collectives, entering(): everything = jax.tree.map(lambda part: lax.all_gather(part, axis), x)  34.2 us
    select_n x32, other arithmetic, turn(): return jax.tree.map(lambda a, b: jnp.where(reached, a, b), new, before)  31.8 us
    psum x1, blocking collectives, body(): group_sums = lax.psum(jnp.where(own_slot, squares[None, :], 0.0), 'tp')  26.8 us
  transfers between devices with their start and end apart: 6, of which 6 were waited for; matrix products, arithmetic and copies ran while one was open for 4% of the time, Pallas kernels for 0%

commit v1 on v0

--- a/solution.py
+++ b/solution.py
@@ -65,7 +65,9 @@
     group_cols = 2 * STATE
     group_index = lax.axis_index("tp") * heads_dev // (HEADS // GROUPS)
     zx_weight = in_weight.reshape(in_weight.shape[0], 2 * inner_dev)
-    full_weight = lax.all_gather(group_weight, "tp", axis=0, tiled=True)
+    full_weight = jnp.concatenate(
+        lax.all_to_all(jnp.stack([group_weight] * lax.axis_size("tp")), "tp", 0, 0), axis=0
+    )
     map_weight = lax.dynamic_slice_in_dim(full_weight, group_index, 1, 1)[:, 0, :]
     shard_rows = lax.all_gather(hidden, "tp", axis=0, tiled=True)
     projected = jnp.concatenate(

time: 325 us -> 345 us (1.062)
  the two profiles are of different devices: /device:TPU:27 before, /device:TPU:25 now
where the time goes in v1:
time: 345 us; the launch traced here: 344 us
  waiting for transfers between devices  196 us (57%)
  blocking collectives  65.5 us (19%)
  other arithmetic  35.5 us (10%)
  between operations  13.5 us (4%)
  starting transfers between devices  13.4 us (4%)
  local copies, waits for them, and re-layouts  11.4 us (3%)
  matrix products  8.23 us (2%)
    all_gather x1, waiting for transfers between devices, body(): shard_rows = lax.all_gather(hidden, 'tp', axis=0, tiled=True)  61.7 us
    reduce_scatter x1, waiting for transfers between devices, body(): lax.psum_scatter(jnp.dot(normed, out_weight, preferred_element_type=jnp.f...  59.9 us
    all_gather x1, waiting for transfers between devices, entering(): everything = jax.tree.map(lambda part: lax.all_gather(part, axis), x)  48.8 us
    all_gather x1, blocking collectives, entering(): everything = jax.tree.map(lambda part: lax.all_gather(part, axis), x)  38.8 us
    select_n x32, other arithmetic, turn(): return jax.tree.map(lambda a, b: jnp.where(reached, a, b), new, before)  31.8 us
    psum x1, blocking collectives, body(): group_sums = lax.psum(jnp.where(own_slot, squares[None, :], 0.0), 'tp')  26.7 us
    all_to_all x1, waiting for transfers between devices, body(): lax.all_to_all(jnp.stack([group_weight] * lax.axis_size('tp')), 'tp', 0, 0)  24.1 us
    all_to_all x1, starting transfers between devices, body(): lax.all_to_all(jnp.stack([group_weight] * lax.axis_size('tp')), 'tp', 0, 0)  10.3 us
  transfers between devices with their start and end apart: 6, of which 6 were waited for; matrix products, arithmetic and copies ran while one was open for 3% of the time, Pallas kernels for 0%

profile of v1, /device:TPU:25, one launch (start us, length us, event | category | flops | bytes accessed | tf_op | source)
XLA Modules:
  0.0 344.3 jit_solution(17524797760392816426)
XLA Ops:
  6.5 1.2 copy.46
  7.7 2.5 stack.2
  10.2 10.3 %all-to-all-start = ((bf16[16,16,4,2048]{3,1,2,0:T(8,128)(2,1)}), bf16[16,16,4,2048]{3,1,2,0:T(8,128)(2,1)}, u32[]{:S(2)}, u32[]{:S(2)}) async-start(bf16[16,16,4,2048]{3,1,2,0:T(8,128)(2,1)} %stack.2), calls=%async_computation | async-start | bytes 8388608 | tf_op jit(solution)/shard_map/all_to_all | solution.py:69
  20.6 0.7 all-gather.5.cloned.1.call-update
  21.4 1.8 copy.58
  23.2 0.8 dynamic_slice.29
  24.0 0.9 constant_dynamic-slice_fusion
  24.9 61.7 %all-gather.5.cloned.1.call-done = bf16[256,2048]{1,0:T(8,128)(2,1)} async-done(((bf16[16,2048]{1,0:T(8,128)(2,1)}), bf16[256,2048]{1,0:T(8,128)(2,1)}) %all-gather.5.cloned.1.call-update) | async-done | bytes 1048592 | tf_op jit(solution)/shard_map/all_gather | solution.py:72
  86.6 1.6 bitcast_multiply_fusion.1
  88.3 1.2 reduce-window.6
  89.9 2.6 convolution_convert_fusion
  92.6 1.7 collective-permute-start
  94.3 0.2 slice_reduce_fusion
  94.7 0.2 collective-permute-done
  95.0 24.1 %all-to-all-done = bf16[16,16,4,2048]{3,1,2,0:T(8,128)(2,1)} async-done(((bf16[16,16,4,2048]{3,1,2,0:T(8,128)(2,1)}), bf16[16,16,4,2048]{3,1,2,0:T(8,128)(2,1)}, u32[]{:S(2)}, u32[]{:S(2)}) %all-to-all-start) | async-done | bytes 4194336 | tf_op jit(solution)/shard_map/all_to_all | solution.py:69
  119.2 2.5 copy.47
  121.7 0.5 fusion.4
  122.2 1.3 collective-permute-start.1
  123.5 0.2 multiply_convert_fusion.3
  123.8 0.4 collective-permute-done.1
  124.2 0.2 multiply_convert_fusion.4
  124.4 0.8 convolution_add_fusion
  125.5 38.8 %all-gather = f32[32,4,1]{1,2,0:T(1,128)S(1)} all-gather(f32[1,4,1]{1,2,0:T(1,128)S(1)} %copy.50), channel_id=2, replica_groups=mesh['ctx'=32,'tp'=16] {'ctx'}, dimensions={0}, use_global_device_ids=true | all-gather | bytes 528 | tf_op jit(solution)/shard_map/all_gather | solution.py:22
  164.6 0.2 fusion.34
  164.8 48.8 %all-gather.7.cloned.1.call-done = f32[128,64,128]{2,1,0:T(8,128)} async-done(((f32[4,64,128]{2,1,0:T(8,128)}), f32[128,64,128]{2,1,0:T(8,128)}) %all-gather.7.cloned.1.call-update) | async-done | bytes 4194320 | tf_op jit(solution)/shard_map/all_gather | solution.py:22
  213.6 33.0 %while.9 = (s32[]{:T(128)}, f32[4,64,128]{2,1,0:T(8,128)S(1)}, s32[]{:T(128)}, f32[32,4]{1,0:T(8,128)S(1)}, f32[32,4,64,128]{3,2,1,0:T(8,128)}, /*index=5*/s32[]{:T(128)}, s32[]{:T(128)}) while((s32[]{:T(128)}, f32[4,64,128]{2,1,0:T(8,128)S(1)}, s32[]{:T(128)}, f32[32,4]{1,0:T(8,128)S(1)}, f32[32,4,64,128]{3,2,1,0:T(8,128)}, ...), condition=%wide.region_3.4_spmd.clone, body=%wide.region_2.3_spmd.clone.sunk | while | flops 131076 | bytes 393369 | solution.py:32
  213.6 1.0 fusion.52
  214.6 1.0 fusion.52
  215.6 1.0 fusion.52
  216.7 1.0 fusion.52
  217.7 1.0 fusion.52
  218.7 1.0 fusion.52
  219.8 1.0 fusion.52
  220.8 1.0 fusion.52
  221.8 1.0 fusion.52
  222.9 1.0 fusion.52
  223.9 1.0 fusion.52
  224.9 1.0 fusion.52
  226.0 1.0 fusion.52
  227.0 1.0 fusion.52
  228.0 1.0 fusion.52
  229.1 1.0 fusion.52
  230.1 1.0 fusion.52
  231.1 1.0 fusion.52
  232.2 1.0 fusion.52
  233.2 1.0 fusion.52
  234.2 1.0 fusion.52
  235.3 1.0 fusion.52
  236.3 1.0 fusion.52
  237.3 1.0 fusion.52
  238.4 1.0 fusion.52
  239.4 1.0 fusion.52
  240.4 1.0 fusion.52
  241.5 1.0 fusion.52
  242.5 1.0 fusion.52
  243.5 1.0 fusion.52
  244.6 1.0 fusion.52
  245.6 1.0 fusion.52
  246.6 0.2 fusion.1
  246.8 0.5 fusion.3
  247.7 26.7 %psum.7 = f32[4,256]{1,0:T(4,128)S(1)} all-reduce(f32[4,256]{1,0:T(4,128)S(1)} %broadcast_select_fusion), channel_id=1, replica_groups=mesh['ctx'=32,'tp'=16] {'tp'}, use_global_device_ids=true, to_apply=%region_5.6 | all-reduce | flops 1024 | bytes 8192 | tf_op jit(solution)/shard_map/psum | solution.py:148
  274.5 1.8 fusion.27
  276.4 59.9 %reduce-scatter.2.cloned.1.call-done = f32[16,2048]{1,0:T(8,128)} async-done(((f32[256,2048]{1,0:T(8,128)}), f32[16,2048]{1,0:T(8,128)}) %reduce-scatter.2.cloned.1.call-update) | async-done | bytes 131088 | tf_op jit(solution)/shard_map/reduce_scatter | solution.py:152
  336.2 1.5 convert_element_type.77
  (92 shorter events, 2.3 us)
Async XLA Ops:
  6.5 268.0 %copy-start = (bf16[256,2048]{1,0:T(8,128)(2,1)S(1)}, bf16[256,2048]{1,0:T(8,128)(2,1)}, u32[]{:S(2)}) copy-start(bf16[256,2048]{1,0:T(8,128)(2,1)} %param.27) | copy-start | bytes 3145732
  10.2 11.1 %copy-start.1 = (bf16[2048,2,256]{2,1,0:T(2,128)(2,1)S(1)}, bf16[2048,2,256]{2,1,0:T(2,128)(2,1)}, u32[]{:S(2)}) copy-start(bf16[2048,2,256]{2,1,0:T(2,128)(2,1)} %param.16) | copy-start | bytes 6291460
  10.2 108.9 %all-to-all-start = ((bf16[16,16,4,2048]{3,1,2,0:T(8,128)(2,1)}), bf16[16,16,4,2048]{3,1,2,0:T(8,128)(2,1)}, u32[]{:S(2)}, u32[]{:S(2)}) async-start(bf16[16,16,4,2048]{3,1,2,0:T(8,128)(2,1)} %stack.2), calls=%async_computation | async-start | bytes 8388608 | tf_op jit(solution)/shard_map/all_to_all | solution.py:69
  20.5 4.3 %copy-start.7 = (f32[4]{0:T(128)S(1)}, f32[4]{0:T(128)}, u32[]{:S(2)}) copy-start(f32[4]{0:T(128)} %param.24) | copy-start | bytes 52
  20.5 4.4 %copy-start.3 = (f32[4,256]{1,0:T(4,128)S(1)}, f32[4,256]{1,0:T(4,128)}, u32[]{:S(2)}) copy-start(f32[4,256]{1,0:T(4,128)} %param.19) | copy-start | bytes 12292
  20.5 66.1 %copy-start.6 = (bf16[2048,4]{0,1:T(4,128)(2,1)S(1)}, bf16[2048,4]{0,1:T(4,128)(2,1)}, u32[]{:S(2)}) copy-start(bf16[2048,4]{0,1:T(4,128)(2,1)} %param.17) | copy-start | bytes 49156
  20.5 66.1 %copy-start.8 = (f32[4]{0:T(128)S(1)}, f32[4]{0:T(128)}, u32[]{:S(2)}) copy-start(f32[4]{0:T(128)} %param.23) | copy-start | bytes 52
  20.6 66.1 %all-gather.5.cloned.1.call-start = ((), (), s32[]{:S(2)}) async-start(), calls=%async_computation.2 | async-start | bytes 1114112 | tf_op jit(solution)/shard_map/all_gather | solution.py:72
  21.3 192.3 %all-gather.7.cloned.1.call-start = ((), (), s32[]{:S(2)}) async-start(), calls=%async_computation.4 | async-start | bytes 4325376 | tf_op jit(solution)/shard_map/all_gather | solution.py:22
  92.6 2.4 collective-permute-start
  95.0 26.7 %copy-start.2 = (bf16[256,2048]{1,0:T(8,128)(2,1)S(1)}, bf16[256,2048]{1,0:T(8,128)(2,1)}, u32[]{:S(2)}) copy-start(bf16[256,2048]{1,0:T(8,128)(2,1)} %all-gather.5.cloned.1.call-done) | copy-start | bytes 3145732
  95.0 28.5 %copy-start.5 = (f32[256]{0:T(256)S(1)}, f32[256]{0:T(256)}, u32[]{:S(2)}) copy-start(f32[256]{0:T(256)} %param.20) | copy-start | bytes 3076
  122.2 124.7 %copy-start.9 = (f32[4]{0:T(128)S(1)}, f32[4]{0:T(128)}, u32[]{:S(2)}) copy-start(f32[4]{0:T(128)} %param.25) | copy-start | bytes 52
  122.2 2.0 collective-permute-start.1
  124.2 150.3 %copy-start.4 = (f32[256]{0:T(256)S(1)}, f32[256]{0:T(256)}, u32[]{:S(2)}) copy-start(f32[256]{0:T(256)} %param.26) | copy-start | bytes 3076
  125.3 211.0 %reduce-scatter.2.cloned.1.call-start = ((), (), s32[]{:S(2)}) async-start(), calls=%async_computation.3 | async-start | bytes 2228224 | tf_op jit(solution)/shard_map/reduce_scatter | solution.py:152
Sparse Core Ops, SparseCore 0:
  23.5 63.0 all-gather.4
  125.4 88.1 all-gather.6
  276.5 59.7 reduce-scatter.1
